TPU v7x, 128 devices: a whole 4x4x4 slice. The times are simulated.
128 devices in a mesh: req: 32 (over x, z, core), tensor: 4 (over y).
Axes of the slice: x: 4, y: 4, z: 4, core: 2. Of those that a mesh axis runs over, the one named last changes fastest.
Arguments:
- hidden_in: bfloat16 [32768, 2048], P('req', 'tensor'), may hold values from -6 to 6
- segment: int32 [32768], P('req'), may hold values from 0 to 15, never falling along the last dimension, each value on 1 to 4096 neighbouring positions
- w_query: bfloat16 [2048, 1024], P(None, 'tensor'), may hold values from -0.125 to 0.125
- w_key: bfloat16 [2048, 1024], P(None, 'tensor'), may hold values from -0.125 to 0.125
- w_value: bfloat16 [2048, 2048], P(None, 'tensor'), may hold values from -0.125 to 0.125
- w_outgate: bfloat16 [2048, 2048], P(None, 'tensor'), may hold values from -0.125 to 0.125
- w_gate_down: bfloat16 [2048, 16], replicated, may hold values from -0.125 to 0.125
- w_gate_up: bfloat16 [16, 1024], P(None, 'tensor'), may hold values from -1.5 to 1.5
- gate_bias: float32 [1024], P('tensor'), may hold values from -2 to 8
- norm_gain: float32 [512], replicated, may hold values from 0.5 to 1.5
- w_out: bfloat16 [2048, 2048], P('tensor'), may hold values from -0.125 to 0.125
Outputs:
- mixed: bfloat16 [32768, 2048], P('req', 'tensor')
Inputs may be any that keep to these rules, and one draw needn't show every extreme that they name: segment never falls along the tokens; each prompt covers 1 to 4096 consecutive tokens and one covers exactly 4096.
All inputs are finite; a program needn't handle non-finite values.
Results may differ from a plain program's by a relative error of at most 0.014.
Values may be sent and summed in bfloat16 or wider, within the bound.
No kernel may reach another device: no remote copies, remote signals or barrier semaphores. Data moves between devices by JAX's collectives and lax.ppermute only.
A program may use at most 128 MiB of HBM per device.

v0:
```python
import jax
import jax.numpy as jnp
from jax import lax
from jax.sharding import PartitionSpec as P

GROUP = 64
PIECES = 4
SEG_MOST = 4096
HIGHEST = lax.Precision.HIGHEST


def shifted(x, axis, shift, devices):
    pairs = [(i, i + shift) for i in range(devices - shift)]
    return lax.ppermute(x, axis, pairs)


def body(
    hidden_in,
    segment,
    w_query,
    w_key,
    w_value,
    w_outgate,
    w_gate_down,
    w_gate_up,
    gate_bias,
    norm_gain,
    w_out,
):
    tok_rows = hidden_in.shape[0]
    key_width = w_query.shape[1]
    value_width = w_value.shape[1]
    weights = (w_query, w_key, w_value, w_outgate, w_gate_down)
    piece_rows = tok_rows // PIECES
    piece_blocks = piece_rows // GROUP
    blocks = tok_rows // GROUP
    positions = jnp.arange(GROUP)
    causal = positions[None, :] <= positions[:, None]
    starts = jnp.concatenate(
        [jnp.zeros((1,), jnp.int32), (segment[1:] != segment[:-1]).astype(jnp.int32)]
    )
    live_device = (jnp.cumsum(starts) == 0).astype(jnp.float32)
    seg_all = segment.reshape(blocks, GROUP)
    live_all = (jnp.cumsum(starts.reshape(blocks, GROUP), axis=1) == 0).astype(jnp.float32)
    parts = []
    for p in range(PIECES):
        rows = slice(p * piece_rows, (p + 1) * piece_rows)
        piece = lax.all_gather(hidden_in[rows], "tensor", axis=1, tiled=True)
        query_sum, key_sum, value_sum, outgate, low = tuple(
            (jnp.dot(piece, weight, preferred_element_type=jnp.float32) for weight in weights)
        )
        query = query_sum.astype(jnp.bfloat16)
        key = key_sum.astype(jnp.bfloat16)
        value = value_sum.astype(jnp.bfloat16)
        pre_gate = jnp.dot(low, w_gate_up.astype(jnp.float32), precision=HIGHEST) + gate_bias
        logdecay = jax.nn.log_sigmoid(pre_gate) / 16.0
        chunks = slice(p * piece_blocks, (p + 1) * piece_blocks)
        seg_blocks = seg_all[chunks]
        live_blocks = live_all[chunks]
        cumul = jnp.cumsum(logdecay.reshape(piece_blocks, GROUP, key_width), axis=1)
        q_float = query.astype(jnp.float32).reshape(piece_blocks, GROUP, key_width)
        k_float = key.astype(jnp.float32).reshape(piece_blocks, GROUP, key_width)
        v_float = value.astype(jnp.float32).reshape(piece_blocks, GROUP, value_width)
        centre = cumul[:, GROUP // 2, :]
        q_scaled = q_float * jnp.exp(cumul - centre[:, None, :])
        k_scaled = k_float * jnp.exp(centre[:, None, :] - cumul)
        raw_scores = jnp.einsum("ncd,nsd->ncs", q_scaled, k_scaled, precision=HIGHEST)
        allowed = causal[None] & (seg_blocks[:, :, None] == seg_blocks[:, None, :])
        scores = jnp.where(allowed, raw_scores, 0.0)
        intra = jnp.einsum("ncs,nsv->ncv", scores, v_float, precision=HIGHEST)
        block_totals = cumul[:, -1, :]
        same_last = (seg_blocks == seg_blocks[:, -1:]).astype(jnp.float32)
        k_decayed = k_float * jnp.exp(block_totals[:, None, :] - cumul) * same_last[:, :, None]
        chunk_states = jnp.einsum("ncd,ncv->ndv", k_decayed, v_float, precision=HIGHEST)
        chunk_decay = jnp.exp(block_totals) * live_blocks[:, -1:]
        parts.append(
            (
                query,
                outgate,
                q_float,
                cumul,
                live_blocks,
                intra,
                chunk_states,
                chunk_decay,
                block_totals,
            )
        )
    entering = jnp.zeros((key_width, value_width), jnp.float32)
    local_outs = []
    for p in range(PIECES):
        query, outgate, q_float, cumul, live_blocks, intra, chunk_states, chunk_decay, _ = parts[p]
        states = []
        for n in range(piece_blocks):
            states.append(entering)
            entering = chunk_decay[n][:, None] * entering + chunk_states[n]
        inter = (
            jnp.einsum(
                "ncd,ndv->ncv", q_float * jnp.exp(cumul), jnp.stack(states), precision=HIGHEST
            )
            * live_blocks[:, :, None]
        )
        local_outs.append((intra + inter).reshape(piece_rows, value_width))
    final_state = entering
    block_totals = jnp.concatenate([part[8] for part in parts])
    before = jnp.cumsum(block_totals, axis=0) - block_totals
    cumul = jnp.concatenate([part[3] for part in parts])
    device_cumul = (cumul + before[:, None, :]).reshape(tok_rows, key_width)
    devices = lax.axis_size("req")
    window = min(devices - 1, -(-SEG_MOST // tok_rows))
    first_id = (segment[0] + 1).astype(jnp.float32)
    last_id = (segment[-1] + 1).astype(jnp.float32)
    decay_device = jnp.exp(device_cumul[-1]) * live_device[-1]
    tail = jnp.zeros((2, value_width), jnp.float32)
    tail = tail.at[0, :key_width].set(decay_device).at[1, 0].set(first_id).at[1, 1].set(last_id)
    message = jnp.concatenate([final_state, tail]).astype(jnp.bfloat16)
    got = [shifted(message, "req", j, devices).astype(jnp.float32) for j in range(1, window + 1)]
    state_in = got[-1][:key_width]
    last_far = got[-1][key_width + 1, 1]
    for j in range(window - 1, 0, -1):
        msg = got[j - 1]
        link = (msg[key_width + 1, 0] == last_far).astype(jnp.float32)
        state_in = msg[:key_width] + (link * msg[key_width, :key_width])[:, None] * state_in
        last_far = msg[key_width + 1, 1]
    linked = (first_id == last_far).astype(jnp.float32)
    mask = live_device * linked
    outs = []
    for p in range(PIECES):
        rows = slice(p * piece_rows, (p + 1) * piece_rows)
        query, outgate = (parts[p][0], parts[p][1])
        carried = jnp.dot(
            query.astype(jnp.float32) * jnp.exp(device_cumul[rows]), state_in, precision=HIGHEST
        )
        attn = (local_outs[p] + carried * mask[rows][:, None]) * key_width ** (-0.5)
        normed = attn * lax.rsqrt(jnp.mean(attn * attn, axis=-1, keepdims=True) + 1e-05) * norm_gain
        gated = (normed * jax.nn.silu(outgate)).astype(jnp.bfloat16)
        head_term = jnp.dot(gated, w_out, preferred_element_type=jnp.float32)
        outs.append(
            lax.psum_scatter(
                head_term.astype(jnp.bfloat16), "tensor", scatter_dimension=1, tiled=True
            )
        )
    return jnp.concatenate(outs, axis=0)


def solution(mesh):
    in_specs = (
        P("req", "tensor"),
        P("req"),
        P(None, "tensor"),
        P(None, "tensor"),
        P(None, "tensor"),
        P(None, "tensor"),
        P(),
        P(None, "tensor"),
        P("tensor"),
        P(),
        P("tensor", None),
    )
    out_specs = P("req", "tensor")
    return jax.shard_map(body, mesh=mesh, in_specs=in_specs, out_specs=out_specs, check_vma=False)
```

profile of v0, /device:TPU:0, one launch (start us, length us, event | category | flops | bytes accessed | tf_op | source)
XLA Modules:
  0.0 292.2 jit_solution(15862725786038252527)
XLA Ops:
  6.6 2.3 fusion.172
  19.7 16.0 %all-gather.5.cloned.1.call-done = bf16[256,2048]{1,0:T(8,128)(2,1)} async-done(((bf16[256,512]{1,0:T(8,128)(2,1)}), bf16[256,2048]{1,0:T(8,128)(2,1)}) %all-gather.5.cloned.1.call-update) | async-done | bytes 1048592 | tf_op jit(solution)/shard_map/all_gather | solution.py:48
  35.7 1.6 fusion.194
  38.7 23.2 %all-gather.7.cloned.1.call-done = bf16[256,2048]{1,0:T(8,128)(2,1)} async-done(((bf16[256,512]{1,0:T(8,128)(2,1)}), bf16[256,2048]{1,0:T(8,128)(2,1)}) %all-gather.7.cloned.1.call-update) | async-done | bytes 1048592 | tf_op jit(solution)/shard_map/all_gather | solution.py:48
  61.8 1.6 fusion.196
  64.7 23.2 %all-gather.11.cloned.1.call-done = bf16[256,2048]{1,0:T(8,128)(2,1)} async-done(((bf16[256,512]{1,0:T(8,128)(2,1)}), bf16[256,2048]{1,0:T(8,128)(2,1)}) %all-gather.11.cloned.1.call-update) | async-done | bytes 1048592 | tf_op jit(solution)/shard_map/all_gather | solution.py:48
  88.0 1.6 fusion.198
  92.2 21.8 %all-gather.9.cloned.1.call-done = bf16[256,2048]{1,0:T(8,128)(2,1)} async-done(((bf16[256,512]{1,0:T(8,128)(2,1)}), bf16[256,2048]{1,0:T(8,128)(2,1)}) %all-gather.9.cloned.1.call-update) | async-done | bytes 1048592 | tf_op jit(solution)/shard_map/all_gather | solution.py:48
  114.0 1.6 fusion.197
  118.4 1.1 slice_exponential_fusion.3
  121.7 1.2 fusion.82
  124.3 1.2 fusion.88
  126.8 1.2 fusion.91
  129.5 1.2 fusion.85
  130.8 3.8 %multiply_add_fusion = (f32[1,256,512]{2,1,0:T(8,128)}, f32[1,256,512]{2,1,0:T(8,128)}, f32[1,256,512]{2,1,0:T(8,128)}, f32[1,256,512]{2,1,0:T(8,128)}, f32[1,25...) fusion(f32[4,256,512]{2,1,0:T(8,128)S(1)} %fusion.91, ...), kind=kLoop, calls=%fused_computation.127 | loop fusion | flops 3801088 | bytes 15744000 | tf_op jit(solution)/shard_map/add | solution.py:96
  134.7 1.5 fusion.65
  136.2 1.2 scatter.11
  137.4 1.3 scatter.14
  138.6 1.0 pad_maximum_fusion.1
  139.7 5.2 %collective-permute-start.3 = (bf16[258,512]{1,0:T(8,128)(2,1)S(1)}, bf16[258,512]{1,0:T(8,128)(2,1)S(1)}, u32[]{:S(2)}, u32[]{:S(2)}) collective-permute-start(bf16[258,512]{1,0:T(8,128)(2,1)S(1)} %pad_maximum_fusion.1), channel_id=1, source_target_pairs={{0,16},{4,20},{8,24},{12,28},{16,32},{20,36},{24,40},{28,44},{32,4... | collective-permute-start | bytes 792584 | tf_op jit(solution)/shard_map/ppermute | solution.py:14
  144.9 1.3 collective-permute-start.2
  146.2 2.6 collective-permute-start.1
  148.8 4.5 %collective-permute-start = (bf16[258,512]{1,0:T(8,128)(2,1)S(1)}, bf16[258,512]{1,0:T(8,128)(2,1)S(1)}, u32[]{:S(2)}, u32[]{:S(2)}) collective-permute-start(bf16[258,512]{1,0:T(8,128)(2,1)S(1)} %pad_maximum_fusion.1), channel_id=1, source_target_pairs={{0,4},{4,8},{8,12},{12,16},{16,20},{20,24},{24,28},{28,32},{32,36}... | collective-permute-start | bytes 792584 | tf_op jit(solution)/shard_map/ppermute | solution.py:14
  153.4 2.4 bitcast_multiply_fusion
  156.3 1.4 fusion.31
  157.7 1.1 convolution_add_fusion
  168.7 1.0 convert_element_type.190
  169.8 1.0 convert_element_type.187
  170.8 1.1 convert_element_type.186
  172.2 0.8 copy-done.3
  173.0 1.5 multiply_reduce_fusion
  175.0 4.4 %convolution_convert_fusion = bf16[256,2048]{1,0:T(8,128)(2,1)} fusion(bf16[512,2048]{1,0:T(8,128)(2,1)S(1)} %copy-done, f32[256,512]{1,0:T(8,128)} %get-tuple-element.117, f32[256]{0:T(256)} %rsqrt_multiply_fusion, f32[512]{0:T(512)} %param.26, bf16[256,2048]{1,0:T(8,128)(2,1)} %all-gather.11.cloned.1.call-done, bf16[2048,512]{1,0:T(8,128)(2,1)} %param.22), kind=kOutput, calls=%fused_computation | convolution fusion | flops 1075314688 | bytes 6818816 | tf_op jit(solution)/shard_map/dot_general | solution.py:137
  179.5 1.9 bitcast_multiply_fusion.1
  181.5 2.1 fusion.34
  184.7 1.5 multiply_reduce_fusion.1
  186.7 4.4 %convolution_convert_fusion.1 = bf16[256,2048]{1,0:T(8,128)(2,1)} fusion(bf16[512,2048]{1,0:T(8,128)(2,1)S(1)} %copy-done, f32[256,512]{1,0:T(8,128)} %get-tuple-element.121, f32[256]{0:T(256)} %rsqrt_multiply_fusion.1, f32[512]{0:T(512)} %param.26, bf16[256,2048]{1,0:T(8,128)(2,1)} %all-gather.9.cloned.1.call-done, bf16[2048,512]{1,0:T(8,128)(2,1)} %param.22), kind=kOutput, calls=%fused_computation.1 | convolution fusion | flops 1075314688 | bytes 6818816 | tf_op jit(solution)/shard_map/dot_general | solution.py:137
  191.5 1.8 bitcast_multiply_fusion.2
  193.4 2.1 fusion.37
  196.6 1.5 multiply_reduce_fusion.2
  198.1 4.4 %convolution_convert_fusion.2 = bf16[256,2048]{1,0:T(8,128)(2,1)} fusion(bf16[512,2048]{1,0:T(8,128)(2,1)S(1)} %copy-done, f32[256,512]{1,0:T(8,128)} %get-tuple-element.125, f32[256]{0:T(256)S(1)} %rsqrt_multiply_fusion.2, f32[512]{0:T(512)S(1)} %copy-done.102, bf16[256,2048]{1,0:T(8,128)(2,1)} %all-gather.7.cloned.1.call-done, bf16[2048,512]{1,0:T(8,128)(2,1)} %param.22), kind=kOutput, calls=%fused_computation.2 | convolution fusion | flops 1075314688 | bytes 6818816 | tf_op jit(solution)/shard_map/dot_general | solution.py:137
  202.6 1.8 bitcast_multiply_fusion.3
  205.4 1.4 fusion.43
  206.8 1.5 multiply_reduce_fusion.3
  208.3 4.1 %convolution_convert_fusion.3 = bf16[256,2048]{1,0:T(8,128)(2,1)} fusion(bf16[512,2048]{1,0:T(8,128)(2,1)S(1)} %copy-done, f32[256,512]{1,0:T(8,128)} %get-tuple-element.129, f32[512]{0:T(512)S(1)} %copy-done.103, f32[256]{0:T(256)S(1)} %rsqrt_multiply_fusion.3, bf16[256,2048]{1,0:T(8,128)(2,1)S(1)} %copy-done.8, bf16[2048,512]{1,0:T(8,128)(2,1)} %param.22), kind=kOutput, calls=%fused_computation.3 | convolution fusion | flops 1075314688 | bytes 6818816 | tf_op jit(solution)/shard_map/dot_general | solution.py:137
  212.4 18.9 %reduce-scatter.9.cloned.1.call-done = bf16[256,512]{1,0:T(8,128)(2,1)} async-done(((bf16[256,2048]{1,0:T(8,128)(2,1)}), bf16[256,512]{1,0:T(8,128)(2,1)}) %reduce-scatter.9.cloned.1.call-update) | async-done | bytes 262160 | tf_op jit(solution)/shard_map/reduce_scatter | solution.py:139
  231.3 25.9 %reduce-scatter.7.cloned.1.call-done = bf16[256,512]{1,0:T(8,128)(2,1)} async-done(((bf16[256,2048]{1,0:T(8,128)(2,1)}), bf16[256,512]{1,0:T(8,128)(2,1)}) %reduce-scatter.7.cloned.1.call-update) | async-done | bytes 262160 | tf_op jit(solution)/shard_map/reduce_scatter | solution.py:139
  257.2 25.9 %reduce-scatter.5.cloned.1.call-done = bf16[256,512]{1,0:T(8,128)(2,1)} async-done(((bf16[256,2048]{1,0:T(8,128)(2,1)}), bf16[256,512]{1,0:T(8,128)(2,1)}) %reduce-scatter.5.cloned.1.call-update) | async-done | bytes 262160 | tf_op jit(solution)/shard_map/reduce_scatter | solution.py:139
  283.1 2.2 pad_maximum_fusion
  (321 shorter events, 33.6 us)
Async XLA Ops:
  6.5 168.5 %copy-start = (bf16[512,2048]{1,0:T(8,128)(2,1)S(1)}, bf16[512,2048]{1,0:T(8,128)(2,1)}, u32[]{:S(2)}) copy-start(bf16[512,2048]{1,0:T(8,128)(2,1)} %param.27) | copy-start | bytes 6291460
  6.5 4.5 %copy-start.69 = (s32[1024]{0:T(1024)S(1)}, s32[1024]{0:T(1024)}, u32[]{:S(2)}) copy-start(s32[1024]{0:T(1024)} %param.18) | copy-start | bytes 12292
  6.5 29.2 %copy-start.27 = (bf16[2048,16]{0,1:T(8,128)(2,1)S(1)}, bf16[2048,16]{0,1:T(8,128)(2,1)}, u32[]{:S(2)}) copy-start(bf16[2048,16]{0,1:T(8,128)(2,1)} %param.23) | copy-start | bytes 196612
  6.5 30.8 %copy-start.104 = (f32[256]{0:T(256)S(1)}, f32[256]{0:T(256)}, u32[]{:S(2)}) copy-start(f32[256]{0:T(256)} %param.25) | copy-start | bytes 3076
  6.5 30.8 %copy-start.101 = (bf16[16,256]{1,0:T(8,128)(2,1)S(1)}, bf16[16,256]{1,0:T(8,128)(2,1)}, u32[]{:S(2)}) copy-start(bf16[16,256]{1,0:T(8,128)(2,1)} %param.24) | copy-start | bytes 24580
  6.5 29.1 %all-gather.5.cloned.1.call-start = ((), (), s32[]{:S(2)}) async-start(), calls=%async_computation.4 | async-start | bytes 1310720 | tf_op jit(solution)/shard_map/all_gather | solution.py:48
  8.9 52.9 %all-gather.7.cloned.1.call-start = ((), (), s32[]{:S(2)}) async-start(), calls=%async_computation.5 | async-start | bytes 1310720 | tf_op jit(solution)/shard_map/all_gather | solution.py:48
  9.7 78.3 %all-gather.11.cloned.1.call-start = ((), (), s32[]{:S(2)}) async-start(), calls=%async_computation.7 | async-start | bytes 1310720 | tf_op jit(solution)/shard_map/all_gather | solution.py:48
  10.4 103.6 %all-gather.9.cloned.1.call-start = ((), (), s32[]{:S(2)}) async-start(), calls=%async_computation.6 | async-start | bytes 1310720 | tf_op jit(solution)/shard_map/all_gather | solution.py:48
  11.0 201.4 %reduce-scatter.11.cloned.1.call-start = ((), (), s32[]{:S(2)}) async-start(), calls=%async_computation.11 | async-start | bytes 1310720 | tf_op jit(solution)/shard_map/reduce_scatter | solution.py:139
  14.3 3.5 %copy-start.61 = (s32[4,64]{1,0:T(4,128)}, s32[4,64]{1,0:T(4,128)S(1)}, u32[]{:S(2)}) copy-start(s32[4,64]{1,0:T(4,128)S(1)} %eq.130) | copy-start | bytes 3076
  16.1 19.6 %copy-start.63 = (s32[4,64]{1,0:T(4,128)}, s32[4,64]{1,0:T(4,128)S(1)}, u32[]{:S(2)}) copy-start(s32[4,64]{1,0:T(4,128)S(1)} %slice.469) | copy-start | bytes 3076
  16.9 18.8 %copy-start.67 = (s32[4,64]{1,0:T(4,128)}, s32[4,64]{1,0:T(4,128)S(1)}, u32[]{:S(2)}) copy-start(s32[4,64]{1,0:T(4,128)S(1)} %slice.485) | copy-start | bytes 3076
  18.1 17.6 %copy-start.59 = (s32[8,128]{1,0:T(8,128)}, s32[8,128]{1,0:T(8,128)S(1)}, u32[]{:S(2)}) copy-start(s32[8,128]{1,0:T(8,128)S(1)} %reduce-window.9) | copy-start | bytes 12292
  18.3 17.4 %copy-start.93 = (s32[8]{0:T(128)}, s32[8]{0:T(128)S(1)}, u32[]{:S(2)}) copy-start(s32[8]{0:T(128)S(1)} %slice_reduce_fusion) | copy-start | bytes 100
  38.0 83.6 %copy-start.16 = (f32[4,64,256]{2,1,0:T(8,128)}, f32[4,64,256]{2,1,0:T(8,128)S(1)}, u32[]{:S(2)}) copy-start(f32[4,64,256]{2,1,0:T(8,128)S(1)} %reduce_window_sum.64) | copy-start | bytes 786436
  90.3 36.5 %copy-start.14 = (f32[4,64,256]{2,1,0:T(8,128)}, f32[4,64,256]{2,1,0:T(8,128)S(1)}, u32[]{:S(2)}) copy-start(f32[4,64,256]{2,1,0:T(8,128)S(1)} %reduce_window_sum.68) | copy-start | bytes 786436
  90.9 27.5 %copy-start.55 = (f32[4,1,256]{2,0,1:T(4,128)}, f32[4,1,256]{2,0,1:T(4,128)S(1)}, u32[]{:S(2)}) copy-start(f32[4,1,256]{2,0,1:T(4,128)S(1)} %copy.57) | copy-start | bytes 12292
  116.3 7.9 %copy-start.12 = (f32[4,64,256]{2,1,0:T(8,128)}, f32[4,64,256]{2,1,0:T(8,128)S(1)}, u32[]{:S(2)}) copy-start(f32[4,64,256]{2,1,0:T(8,128)S(1)} %reduce_window_sum.67) | copy-start | bytes 786436
  130.8 3.8 %copy-start.96 = (f32[1,256]{1,0:T(1,128)S(1)}, f32[1,256]{1,0:T(1,128)}, u32[]{:S(2)}) copy-start(f32[1,256]{1,0:T(1,128)} %get-tuple-element.90) | copy-start | bytes 3076
  134.6 18.7 %copy-start.73 = (f32[4,1,256]{2,1,0:T(1,128)S(1)}, f32[4,1,256]{2,1,0:T(1,128)}, u32[]{:S(2)}) copy-start(f32[4,1,256]{2,1,0:T(1,128)} %get-tuple-element.80) | copy-start | bytes 12292
  134.7 18.7 %copy-start.2 = (bf16[2048,256]{1,0:T(8,128)(2,1)S(1)}, bf16[2048,256]{1,0:T(8,128)(2,1)}, u32[]{:S(2)}) copy-start(bf16[2048,256]{1,0:T(8,128)(2,1)} %param.19) | copy-start | bytes 3145732
  136.2 19.6 %copy-start.68 = (s32[4,64]{1,0:T(4,128)S(1)}, s32[4,64]{1,0:T(4,128)}, u32[]{:S(2)}) copy-start(s32[4,64]{1,0:T(4,128)} %copy-done.67) | copy-start | bytes 3076
  138.6 17.2 %copy-start.15 = (f32[4,64,256]{2,1,0:T(8,128)S(1)}, f32[4,64,256]{2,1,0:T(8,128)}, u32[]{:S(2)}) copy-start(f32[4,64,256]{2,1,0:T(8,128)} %copy-done.14) | copy-start | bytes 786436
  138.6 17.2 %copy-start.24 = (bf16[256,256]{1,0:T(8,128)(2,1)S(1)}, bf16[256,256]{1,0:T(8,128)(2,1)}, u32[]{:S(2)}) copy-start(bf16[256,256]{1,0:T(8,128)(2,1)} %copy-done.23) | copy-start | bytes 393220
  139.6 16.6 %copy-start.46 = (f32[1,256,512]{2,1,0:T(8,128)S(1)}, f32[1,256,512]{2,1,0:T(8,128)}, u32[]{:S(2)}) copy-start(f32[1,256,512]{2,1,0:T(8,128)} %get-tuple-element.45) | copy-start | bytes 1572868
  139.7 16.6 %copy-start.47 = (f32[1,256,512]{2,1,0:T(8,128)S(1)}, f32[1,256,512]{2,1,0:T(8,128)}, u32[]{:S(2)}) copy-start(f32[1,256,512]{2,1,0:T(8,128)} %get-tuple-element.46) | copy-start | bytes 1572868
  139.7 16.6 %copy-start.48 = (f32[1,256,512]{2,1,0:T(8,128)S(1)}, f32[1,256,512]{2,1,0:T(8,128)}, u32[]{:S(2)}) copy-start(f32[1,256,512]{2,1,0:T(8,128)} %get-tuple-element.47) | copy-start | bytes 1572868
  139.7 16.6 %copy-start.49 = (f32[1,256,512]{2,1,0:T(8,128)S(1)}, f32[1,256,512]{2,1,0:T(8,128)}, u32[]{:S(2)}) copy-start(f32[1,256,512]{2,1,0:T(8,128)} %get-tuple-element.48) | copy-start | bytes 1572868
  139.7 16.6 %copy-start.99 = (f32[4,64]{1,0:T(4,128)S(1)}, f32[4,64]{1,0:T(4,128)}, u32[]{:S(2)}) copy-start(f32[4,64]{1,0:T(4,128)} %get-tuple-element.83) | copy-start | bytes 3076
  139.7 19.2 %collective-permute-start.3 = (bf16[258,512]{1,0:T(8,128)(2,1)S(1)}, bf16[258,512]{1,0:T(8,128)(2,1)S(1)}, u32[]{:S(2)}, u32[]{:S(2)}) collective-permute-start(bf16[258,512]{1,0:T(8,128)(2,1)S(1)} %pad_maximum_fusion.1), channel_id=1, source_target_pairs={{0,16},{4,20},{8,24},{12,28},{16,32},{20,36},{24,40},{28,44},{32,4... | collective-permute-start | bytes 792584 | tf_op jit(solution)/shard_map/ppermute | solution.py:14
  144.9 14.7 %collective-permute-start.2 = (bf16[258,512]{1,0:T(8,128)(2,1)S(1)}, bf16[258,512]{1,0:T(8,128)(2,1)S(1)}, u32[]{:S(2)}, u32[]{:S(2)}) collective-permute-start(bf16[258,512]{1,0:T(8,128)(2,1)S(1)} %pad_maximum_fusion.1), channel_id=1, source_target_pairs={{0,12},{4,16},{8,20},{12,24},{16,28},{20,32},{24,36},{28,40},{32,4... | collective-permute-start | bytes 792584 | tf_op jit(solution)/shard_map/ppermute | solution.py:14
  146.2 16.0 %collective-permute-start.1 = (bf16[258,512]{1,0:T(8,128)(2,1)S(1)}, bf16[258,512]{1,0:T(8,128)(2,1)S(1)}, u32[]{:S(2)}, u32[]{:S(2)}) collective-permute-start(bf16[258,512]{1,0:T(8,128)(2,1)S(1)} %pad_maximum_fusion.1), channel_id=1, source_target_pairs={{0,8},{4,12},{8,16},{12,20},{16,24},{20,28},{24,32},{28,36},{32,40... | collective-permute-start | bytes 792584 | tf_op jit(solution)/shard_map/ppermute | solution.py:14
  148.8 16.0 %collective-permute-start = (bf16[258,512]{1,0:T(8,128)(2,1)S(1)}, bf16[258,512]{1,0:T(8,128)(2,1)S(1)}, u32[]{:S(2)}, u32[]{:S(2)}) collective-permute-start(bf16[258,512]{1,0:T(8,128)(2,1)S(1)} %pad_maximum_fusion.1), channel_id=1, source_target_pairs={{0,4},{4,8},{8,12},{12,16},{16,20},{20,24},{24,28},{28,32},{32,36}... | collective-permute-start | bytes 792584 | tf_op jit(solution)/shard_map/ppermute | solution.py:14
  156.3 11.7 %copy-start.60 = (s32[8,128]{1,0:T(8,128)S(1)}, s32[8,128]{1,0:T(8,128)}, u32[]{:S(2)}) copy-start(s32[8,128]{1,0:T(8,128)} %copy-done.59) | copy-start | bytes 12292
  156.3 11.7 %copy-start.94 = (s32[8]{0:T(128)S(1)}, s32[8]{0:T(128)}, u32[]{:S(2)}) copy-start(s32[8]{0:T(128)} %copy-done.93) | copy-start | bytes 100
  158.9 7.3 %copy-start.53 = (bf16[258,512]{1,0:T(8,128)(2,1)}, bf16[258,512]{1,0:T(8,128)(2,1)S(1)}, u32[]{:S(2)}) copy-start(bf16[258,512]{1,0:T(8,128)(2,1)S(1)} %collective-permute-done.3) | copy-start | bytes 792580
  168.1 3.9 %copy-start.54 = (bf16[258,512]{1,0:T(8,128)(2,1)S(1)}, bf16[258,512]{1,0:T(8,128)(2,1)}, u32[]{:S(2)}) copy-start(bf16[258,512]{1,0:T(8,128)(2,1)} %copy-done.53) | copy-start | bytes 792580
  175.0 4.5 %copy-start.72 = (f32[4,1,256]{2,1,0:T(1,128)S(1)}, f32[4,1,256]{2,1,0:T(1,128)}, u32[]{:S(2)}) copy-start(f32[4,1,256]{2,1,0:T(1,128)} %get-tuple-element.78) | copy-start | bytes 12292
  179.4 51.9 %reduce-scatter.9.cloned.1.call-start = ((), (), s32[]{:S(2)}) async-start(), calls=%async_computation.10 | async-start | bytes 1310720 | tf_op jit(solution)/shard_map/reduce_scatter | solution.py:139
  186.7 4.8 %copy-start.71 = (f32[4,1,256]{2,1,0:T(1,128)S(1)}, f32[4,1,256]{2,1,0:T(1,128)}, u32[]{:S(2)}) copy-start(f32[4,1,256]{2,1,0:T(1,128)} %get-tuple-element.76) | copy-start | bytes 12292
  191.2 66.1 %reduce-scatter.7.cloned.1.call-start = ((), (), s32[]{:S(2)}) async-start(), calls=%async_computation.9 | async-start | bytes 1310720 | tf_op jit(solution)/shard_map/reduce_scatter | solution.py:139
  198.0 4.5 %copy-start.70 = (f32[4,1,256]{2,1,0:T(1,128)S(1)}, f32[4,1,256]{2,1,0:T(1,128)}, u32[]{:S(2)}) copy-start(f32[4,1,256]{2,1,0:T(1,128)} %get-tuple-element.74) | copy-start | bytes 12292
  202.5 80.7 %reduce-scatter.5.cloned.1.call-start = ((), (), s32[]{:S(2)}) async-start(), calls=%async_computation.8 | async-start | bytes 1310720 | tf_op jit(solution)/shard_map/reduce_scatter | solution.py:139
  202.6 2.8 copy-start.35
  202.6 2.8 copy-start.36
  205.4 2.9 %copy-start.8 = (bf16[256,2048]{1,0:T(8,128)(2,1)S(1)}, bf16[256,2048]{1,0:T(8,128)(2,1)}, u32[]{:S(2)}) copy-start(bf16[256,2048]{1,0:T(8,128)(2,1)} %all-gather.5.cloned.1.call-done) | copy-start | bytes 3145732
  205.4 2.9 copy-start.103
  (69 other events, 112.7 us)
Sparse Core Ops, SparseCore 0:
  9.1 26.5 all-gather.4
  37.4 24.4 all-gather.6
  63.5 24.4 all-gather.10
  89.5 24.4 all-gather.8
  179.5 25.9 reduce-scatter.10
  207.8 23.4 reduce-scatter.8
  233.7 23.4 reduce-scatter.6
  259.6 23.4 reduce-scatter.4
where the time goes:
time: 293 us; the launch traced here: 292 us
  waiting for transfers between devices  157 us (54%)
  matrix products  59.7 us (20%)
  between operations  21.6 us (7%)
  local copies, waits for them, and re-layouts  21.5 us (7%)
  other arithmetic  18.3 us (6%)
  starting transfers between devices  14.2 us (5%)
    all_gather x4, waiting for transfers between devices, body(): piece = lax.all_gather(hidden_in[rows], 'tensor', axis=1, tiled=True)  84.2 us
    reduce_scatter x4, waiting for transfers between devices, body(): lax.psum_scatter(head_term.astype(jnp.bfloat16), 'tensor', scatter_dimens...  70.7 us
    dot_general x16, matrix products, body(): jnp.dot(piece, weight, preferred_element_type=jnp.float32)  19 us
    dot_general x4, matrix products, body(): head_term = jnp.dot(gated, w_out, preferred_element_type=jnp.float32)  17.3 us
    ppermute x4, starting transfers between devices, shifted(): return lax.ppermute(x, axis, pairs)  13.6 us
    dot_general x4, matrix products, body(): jnp.einsum('ncd,ndv->ncv', q_float * jnp.exp(cumul), jnp.stack(states), p...  7.03 us
  transfers between devices with their start and end apart: 12, of which 7 were waited for; matrix products, arithmetic and copies ran while one was open for 19% of the time, Pallas kernels for 0%

commit v1 on v0

--- a/solution.py
+++ b/solution.py
@@ -2,11 +2,18 @@
 import jax.numpy as jnp
 from jax import lax
 from jax.sharding import PartitionSpec as P
+from jax.lax import all_to_all, axis_size
 
 GROUP = 64
 PIECES = 4
 SEG_MOST = 4096
 HIGHEST = lax.Precision.HIGHEST
+
+
+def _enter_slabs(work_x, out_dim):
+    aux = jnp.stack([work_x for _ in range(axis_size("tensor"))], axis=0)
+    x_next = all_to_all(aux, "tensor", 0, 0)
+    return jnp.concatenate(x_next, out_dim)
 
 
 def shifted(x, axis, shift, devices):
@@ -45,7 +52,7 @@
     parts = []
     for p in range(PIECES):
         rows = slice(p * piece_rows, (p + 1) * piece_rows)
-        piece = lax.all_gather(hidden_in[rows], "tensor", axis=1, tiled=True)
+        piece = _enter_slabs(hidden_in[rows], 1)
         query_sum, key_sum, value_sum, outgate, low = tuple(
             (jnp.dot(piece, weight, preferred_element_type=jnp.float32) for weight in weights)
         )

time: 293 us -> 281 us (0.959)
  waiting for transfers between devices: 157 us -> 94.9 us
  starting transfers between devices: 14.2 us -> 32.3 us
  matrix products: 59.7 us -> 75 us
  local copies, waits for them, and re-layouts: 21.5 us -> 34.2 us
  other arithmetic: 18.3 us -> 22.4 us
    all_gather x4 -> x0, waiting for transfers between devices: 84.2 us -> none  [body(): piece = lax.all_gather(hidden_in[rows], 'tensor', axis=1, tiled=True)]
    all_to_all x0 -> x4, waiting for transfers between devices: none -> 22.9 us  [_enter_slabs(): x_next = all_to_all(aux, 'tensor', 0, 0)]
    all_to_all x0 -> x4, starting transfers between devices: none -> 17.4 us  [_enter_slabs(): x_next = all_to_all(aux, 'tensor', 0, 0)]
    dot_general x16, matrix products: 19 us -> 34.1 us  [body(): jnp.dot(piece, weight, preferred_element_type=jnp.float32)]
    another operation x2 -> x6, local copies, waits for them, and re-layouts: 0.19 us -> 6.24 us  [the longest x4 6.05 us: _enter_slabs(): aux = jnp.stack([work_x for _ in range(axis_size('tensor'))], axis=0)]
    slice x1 -> x5, local copies, waits for them, and re-layouts: 2.32 us -> 6.09 us  [body(): piece = _enter_slabs(hidden_in[rows], 1)]
    squeeze x0 -> x3, local copies, waits for them, and re-layouts: none -> 3.16 us  [body(): block_totals = cumul[:, -1, :]]
  transfers between devices with their start and end apart: 12 -> 12, of which waited for: 7 -> 8; matrix products, arithmetic and copies ran while one was open for 19% -> 24% of each run, Pallas kernels for 0% -> 0%
where the time goes in v1:
time: 281 us; the launch traced here: 280 us
  waiting for transfers between devices  94.9 us (34%)
  matrix products  75 us (27%)
  local copies, waits for them, and re-layouts  34.2 us (12%)
  starting transfers between devices  32.3 us (11%)
  other arithmetic  22.4 us (8%)
  between operations  21 us (7%)
    reduce_scatter x4, waiting for transfers between devices, body(): lax.psum_scatter(head_term.astype(jnp.bfloat16), 'tensor', scatter_dimens...  71.6 us
    dot_general x16, matrix products, body(): jnp.dot(piece, weight, preferred_element_type=jnp.float32)  34.1 us
    all_to_all x4, waiting for transfers between devices, _enter_slabs(): x_next = all_to_all(aux, 'tensor', 0, 0)  22.9 us
    dot_general x4, matrix products, body(): head_term = jnp.dot(gated, w_out, preferred_element_type=jnp.float32)  17.6 us
    all_to_all x4, starting transfers between devices, _enter_slabs(): x_next = all_to_all(aux, 'tensor', 0, 0)  17.4 us
    ppermute x4, starting transfers between devices, shifted(): return lax.ppermute(x, axis, pairs)  14.2 us
    dot_general x4, matrix products, body(): jnp.einsum('ncd,ndv->ncv', q_float * jnp.exp(cumul), jnp.stack(states), p...  6.25 us
    slice x5, local copies, waits for them, and re-layouts, body(): piece = _enter_slabs(hidden_in[rows], 1)  6.09 us
  transfers between devices with their start and end apart: 12, of which 8 were waited for; matrix products, arithmetic and copies ran while one was open for 24% of the time, Pallas kernels for 0%

profile of v1, /device:TPU:0, one launch (start us, length us, event | category | flops | bytes accessed | tf_op | source)
XLA Modules:
  0.0 279.7 jit_solution(17986343779974665119)
XLA Ops:
  6.5 2.2 fusion.172
  10.0 4.6 %all-to-all-start.2 = ((bf16[4,256,512]{1,2,0:T(8,128)(2,1)}), bf16[4,256,512]{1,2,0:T(8,128)(2,1)S(1)}, u32[]{:S(2)}, u32[]{:S(2)}) async-start(bf16[4,256,512]{1,2,0:T(8,128)(2,1)} %stack.19), calls=%async_computation.2 | async-start | bytes 2097152 | tf_op jit(solution)/shard_map/all_to_all | solution.py:15
  21.0 8.6 %all-to-all-done.2 = bf16[4,256,512]{1,2,0:T(8,128)(2,1)S(1)} async-done(((bf16[4,256,512]{1,2,0:T(8,128)(2,1)}), bf16[4,256,512]{1,2,0:T(8,128)(2,1)S(1)}, u32[]{:S(2)}, u32[]{:S(2)}) %all-to-all-start.2) | async-done | bytes 1048608 | tf_op jit(solution)/shard_map/all_to_all | solution.py:15
  31.6 4.4 %all-to-all-start.3 = ((bf16[4,256,512]{1,2,0:T(8,128)(2,1)}), bf16[4,256,512]{1,2,0:T(8,128)(2,1)}, u32[]{:S(2)}, u32[]{:S(2)}) async-start(bf16[4,256,512]{1,2,0:T(8,128)(2,1)} %stack.20), calls=%async_computation.3 | async-start | bytes 2097152 | tf_op jit(solution)/shard_map/all_to_all | solution.py:15
  39.1 1.8 copy.34
  42.4 2.1 fusion.197
  44.4 1.7 convolution_convert_fusion.12
  46.2 4.2 %all-to-all-done.3 = bf16[4,256,512]{1,2,0:T(8,128)(2,1)} async-done(((bf16[4,256,512]{1,2,0:T(8,128)(2,1)}), bf16[4,256,512]{1,2,0:T(8,128)(2,1)}, u32[]{:S(2)}, u32[]{:S(2)}) %all-to-all-start.3) | async-done | bytes 1048608 | tf_op jit(solution)/shard_map/all_to_all | solution.py:15
  50.3 2.0 stack.18
  52.3 4.2 %all-to-all-start.1 = ((bf16[4,256,512]{1,2,0:T(8,128)(2,1)}), bf16[4,256,512]{1,2,0:T(8,128)(2,1)}, u32[]{:S(2)}, u32[]{:S(2)}) async-start(bf16[4,256,512]{1,2,0:T(8,128)(2,1)} %stack.18), calls=%async_computation.1 | async-start | bytes 2097152 | tf_op jit(solution)/shard_map/all_to_all | solution.py:15
  56.6 2.2 fusion.198
  58.8 2.4 convolution_convert_fusion.11
  61.2 1.4 convolution_convert_fusion.5
  62.6 7.4 %all-to-all-done.1 = bf16[4,256,512]{1,2,0:T(8,128)(2,1)} async-done(((bf16[4,256,512]{1,2,0:T(8,128)(2,1)}), bf16[4,256,512]{1,2,0:T(8,128)(2,1)}, u32[]{:S(2)}, u32[]{:S(2)}) %all-to-all-start.1) | async-done | bytes 1048608 | tf_op jit(solution)/shard_map/all_to_all | solution.py:15
  70.0 2.0 stack.16
  72.0 4.2 %all-to-all-start = ((bf16[4,256,512]{1,2,0:T(8,128)(2,1)}), bf16[4,256,512]{1,2,0:T(8,128)(2,1)}, u32[]{:S(2)}, u32[]{:S(2)}) async-start(bf16[4,256,512]{1,2,0:T(8,128)(2,1)} %stack.16), calls=%async_computation | async-start | bytes 2097152 | tf_op jit(solution)/shard_map/all_to_all | solution.py:15
  76.5 1.9 convolution_convert_fusion.13
  78.3 2.1 fusion.196
  80.5 2.7 convolution_convert_fusion.4
  83.1 2.7 convolution_convert_fusion.6
  85.8 2.7 all-to-all-done
  88.5 2.2 fusion.195
  90.7 1.7 convolution_convert_fusion.14
  92.5 2.7 convolution_convert_fusion.7
  103.2 1.9 fusion.94
  119.8 3.6 %multiply_add_fusion = (f32[1,256,512]{2,1,0:T(8,128)}, f32[1,256,512]{2,1,0:T(8,128)}, f32[1,256,512]{2,1,0:T(8,128)}, f32[1,256,512]{2,1,0:T(8,128)}, f32[1,25...) fusion(f32[4,256,512]{2,1,0:T(8,128)S(1)} %fusion.91, ...), kind=kLoop, calls=%fused_computation.127 | loop fusion | flops 3801088 | bytes 15744000 | tf_op jit(solution)/shard_map/add | solution.py:103
  123.5 1.5 fusion.65
  128.7 5.9 %collective-permute-start.3 = (bf16[258,512]{1,0:T(8,128)(2,1)S(1)}, bf16[258,512]{1,0:T(8,128)(2,1)S(1)}, u32[]{:S(2)}, u32[]{:S(2)}) collective-permute-start(bf16[258,512]{1,0:T(8,128)(2,1)S(1)} %pad_maximum_fusion.1), channel_id=1, source_target_pairs={{0,16},{4,20},{8,24},{12,28},{16,32},{20,36},{24,40},{28,44},{32,4... | collective-permute-start | bytes 792584 | tf_op jit(solution)/shard_map/ppermute | solution.py:21
  136.0 2.9 %collective-permute-start.1 = (bf16[258,512]{1,0:T(8,128)(2,1)S(1)}, bf16[258,512]{1,0:T(8,128)(2,1)S(1)}, u32[]{:S(2)}, u32[]{:S(2)}) collective-permute-start(bf16[258,512]{1,0:T(8,128)(2,1)S(1)} %pad_maximum_fusion.1), channel_id=1, source_target_pairs={{0,8},{4,12},{8,16},{12,20},{16,24},{20,28},{24,32},{28,36},{32,40... | collective-permute-start | bytes 792584 | tf_op jit(solution)/shard_map/ppermute | solution.py:21
  138.9 4.0 %collective-permute-start = (bf16[258,512]{1,0:T(8,128)(2,1)S(1)}, bf16[258,512]{1,0:T(8,128)(2,1)S(1)}, u32[]{:S(2)}, u32[]{:S(2)}) collective-permute-start(bf16[258,512]{1,0:T(8,128)(2,1)S(1)} %pad_maximum_fusion.1), channel_id=1, source_target_pairs={{0,4},{4,8},{8,12},{12,16},{16,20},{20,24},{24,28},{28,32},{32,36}... | collective-permute-start | bytes 792584 | tf_op jit(solution)/shard_map/ppermute | solution.py:21
  143.0 2.5 bitcast_multiply_fusion
  161.3 1.5 multiply_reduce_fusion
  163.3 4.5 %convolution_convert_fusion = bf16[256,2048]{1,0:T(8,128)(2,1)} fusion(bf16[512,2048]{1,0:T(8,128)(2,1)S(1)} %copy-done, f32[256,512]{1,0:T(8,128)} %get-tuple-element.117, f32[256]{0:T(256)} %rsqrt_multiply_fusion, f32[512]{0:T(512)} %param.26, bf16[256,2048]{0,1:T(8,128)(2,1)} %bitcast.19, bf16[2048,512]{1,0:T(8,128)(2,1)} %param.22), kind=kOutput, calls=%fused_computation | convolution fusion | flops 1075314688 | bytes 6818816 | tf_op jit(solution)/shard_map/dot_general | solution.py:144
  167.9 1.9 bitcast_multiply_fusion.1
  169.9 2.1 fusion.34
  173.0 1.5 multiply_reduce_fusion.1
  174.5 4.2 %convolution_convert_fusion.1 = bf16[256,2048]{1,0:T(8,128)(2,1)} fusion(bf16[512,2048]{1,0:T(8,128)(2,1)S(1)} %copy-done, f32[256,512]{1,0:T(8,128)} %get-tuple-element.121, f32[256]{0:T(256)S(1)} %rsqrt_multiply_fusion.1, f32[512]{0:T(512)} %param.26, bf16[256,2048]{0,1:T(8,128)(2,1)S(1)} %bitcast.281, bf16[2048,512]{1,0:T(8,128)(2,1)} %param.22), kind=kOutput, calls=%fused_computation.1 | convolution fusion | flops 1075314688 | bytes 6818816 | tf_op jit(solution)/shard_map/dot_general | solution.py:144
  179.0 2.2 bitcast_multiply_fusion.2
  181.3 1.4 fusion.37
  183.8 1.5 multiply_reduce_fusion.2
  185.2 4.6 %convolution_convert_fusion.2 = bf16[256,2048]{1,0:T(8,128)(2,1)} fusion(bf16[512,2048]{1,0:T(8,128)(2,1)S(1)} %copy-done, f32[256,512]{1,0:T(8,128)} %get-tuple-element.125, f32[256]{0:T(256)S(1)} %rsqrt_multiply_fusion.2, f32[512]{0:T(512)S(1)} %copy-done.105, bf16[256,2048]{0,1:T(8,128)(2,1)} %bitcast.13, bf16[2048,512]{1,0:T(8,128)(2,1)} %param.22), kind=kOutput, calls=%fused_computation.2 | convolution fusion | flops 1075314688 | bytes 6818816 | tf_op jit(solution)/shard_map/dot_general | solution.py:144
  189.9 1.9 bitcast_multiply_fusion.3
  192.8 1.4 fusion.43
  195.0 4.4 %convolution_convert_fusion.3 = bf16[256,2048]{1,0:T(8,128)(2,1)} fusion(bf16[512,2048]{1,0:T(8,128)(2,1)S(1)} %copy-done, f32[256,512]{1,0:T(8,128)S(1)} %get-tuple-element.129, f32[512]{0:T(512)S(1)} %copy-done.106, f32[256]{0:T(256)S(1)} %rsqrt_multiply_fusion.3, bf16[256,2048]{0,1:T(8,128)(2,1)} %bitcast.1, bf16[2048,512]{1,0:T(8,128)(2,1)} %param.22), kind=kOutput, calls=%fused_computation.3 | convolution fusion | flops 1075314688 | bytes 6818816 | tf_op jit(solution)/shard_map/dot_general | solution.py:144
  199.4 20.0 %reduce-scatter.9.cloned.1.call-done = bf16[256,512]{1,0:T(8,128)(2,1)} async-done(((bf16[256,2048]{1,0:T(8,128)(2,1)}), bf16[256,512]{1,0:T(8,128)(2,1)}) %reduce-scatter.9.cloned.1.call-update) | async-done | bytes 262160 | tf_op jit(solution)/shard_map/reduce_scatter | solution.py:146
  219.4 25.9 %reduce-scatter.7.cloned.1.call-done = bf16[256,512]{1,0:T(8,128)(2,1)} async-done(((bf16[256,2048]{1,0:T(8,128)(2,1)}), bf16[256,512]{1,0:T(8,128)(2,1)}) %reduce-scatter.7.cloned.1.call-update) | async-done | bytes 262160 | tf_op jit(solution)/shard_map/reduce_scatter | solution.py:146
  245.3 25.7 %reduce-scatter.5.cloned.1.call-done = bf16[256,512]{1,0:T(8,128)(2,1)} async-done(((bf16[256,2048]{1,0:T(8,128)(2,1)}), bf16[256,512]{1,0:T(8,128)(2,1)}) %reduce-scatter.5.cloned.1.call-update) | async-done | bytes 262160 | tf_op jit(solution)/shard_map/reduce_scatter | solution.py:146
  270.9 2.2 pad_maximum_fusion
  (327 shorter events, 55.7 us)
Async XLA Ops:
  6.5 156.7 %copy-start = (bf16[512,2048]{1,0:T(8,128)(2,1)S(1)}, bf16[512,2048]{1,0:T(8,128)(2,1)}, u32[]{:S(2)}) copy-start(bf16[512,2048]{1,0:T(8,128)(2,1)} %param.27) | copy-start | bytes 6291460
  8.8 5.8 %copy-start.68 = (s32[1024]{0:T(1024)S(1)}, s32[1024]{0:T(1024)}, u32[]{:S(2)}) copy-start(s32[1024]{0:T(1024)} %param.18) | copy-start | bytes 12292
  10.0 19.7 %all-to-all-start.2 = ((bf16[4,256,512]{1,2,0:T(8,128)(2,1)}), bf16[4,256,512]{1,2,0:T(8,128)(2,1)S(1)}, u32[]{:S(2)}, u32[]{:S(2)}) async-start(bf16[4,256,512]{1,2,0:T(8,128)(2,1)} %stack.19), calls=%async_computation.2 | async-start | bytes 2097152 | tf_op jit(solution)/shard_map/all_to_all | solution.py:15
  16.5 24.4 %copy-start.62 = (s32[4,64]{1,0:T(4,128)}, s32[4,64]{1,0:T(4,128)S(1)}, u32[]{:S(2)}) copy-start(s32[4,64]{1,0:T(4,128)S(1)} %slice.469) | copy-start | bytes 3076
  16.7 24.1 %copy-start.66 = (s32[4,64]{1,0:T(4,128)}, s32[4,64]{1,0:T(4,128)S(1)}, u32[]{:S(2)}) copy-start(s32[4,64]{1,0:T(4,128)S(1)} %slice.485) | copy-start | bytes 3076
  17.1 23.8 %copy-start.58 = (s32[8,128]{1,0:T(8,128)}, s32[8,128]{1,0:T(8,128)S(1)}, u32[]{:S(2)}) copy-start(s32[8,128]{1,0:T(8,128)S(1)} %reduce-window.9) | copy-start | bytes 12292
  17.3 23.6 %copy-start.94 = (s32[8]{0:T(128)}, s32[8]{0:T(128)S(1)}, u32[]{:S(2)}) copy-start(s32[8]{0:T(128)S(1)} %slice_reduce_fusion) | copy-start | bytes 100
  21.0 21.3 %copy-start.25 = (bf16[2048,16]{0,1:T(8,128)(2,1)S(1)}, bf16[2048,16]{0,1:T(8,128)(2,1)}, u32[]{:S(2)}) copy-start(bf16[2048,16]{0,1:T(8,128)(2,1)} %param.23) | copy-start | bytes 196612
  31.6 9.3 %copy-start.32 = (bf16[256,512]{1,0:T(8,128)(2,1)S(1)}, bf16[256,512]{1,0:T(8,128)(2,1)}, u32[]{:S(2)}) copy-start(bf16[256,512]{1,0:T(8,128)(2,1)} %get-tuple-element.65) | copy-start | bytes 786436
  31.6 12.8 %copy-start.1 = (bf16[2048,256]{1,0:T(8,128)(2,1)S(1)}, bf16[2048,256]{1,0:T(8,128)(2,1)}, u32[]{:S(2)}) copy-start(bf16[2048,256]{1,0:T(8,128)(2,1)} %param.20) | copy-start | bytes 3145732
  31.6 18.7 %all-to-all-start.3 = ((bf16[4,256,512]{1,2,0:T(8,128)(2,1)}), bf16[4,256,512]{1,2,0:T(8,128)(2,1)}, u32[]{:S(2)}, u32[]{:S(2)}) async-start(bf16[4,256,512]{1,2,0:T(8,128)(2,1)} %stack.20), calls=%async_computation.3 | async-start | bytes 2097152 | tf_op jit(solution)/shard_map/all_to_all | solution.py:15
  46.1 69.7 %copy-start.19 = (bf16[256,256]{1,0:T(8,128)(2,1)}, bf16[256,256]{1,0:T(8,128)(2,1)S(1)}, u32[]{:S(2)}) copy-start(bf16[256,256]{1,0:T(8,128)(2,1)S(1)} %convolution_convert_fusion.12) | copy-start | bytes 393220
  52.3 17.7 %all-to-all-start.1 = ((bf16[4,256,512]{1,2,0:T(8,128)(2,1)}), bf16[4,256,512]{1,2,0:T(8,128)(2,1)}, u32[]{:S(2)}, u32[]{:S(2)}) async-start(bf16[4,256,512]{1,2,0:T(8,128)(2,1)} %stack.18), calls=%async_computation.1 | async-start | bytes 2097152 | tf_op jit(solution)/shard_map/all_to_all | solution.py:15
  56.6 4.6 %copy-start.3 = (bf16[4,256,512]{1,2,0:T(8,128)(2,1)S(1)}, bf16[4,256,512]{1,2,0:T(8,128)(2,1)}, u32[]{:S(2)}) copy-start(bf16[4,256,512]{1,2,0:T(8,128)(2,1)} %copy-done.2) | copy-start | bytes 3145732
  56.6 4.6 %copy-start.101 = (bf16[2048,512]{1,0:T(8,128)(2,1)S(1)}, bf16[2048,512]{1,0:T(8,128)(2,1)}, u32[]{:S(2)}) copy-start(bf16[2048,512]{1,0:T(8,128)(2,1)} %param.21) | copy-start | bytes 6291460
  72.0 16.5 %all-to-all-start = ((bf16[4,256,512]{1,2,0:T(8,128)(2,1)}), bf16[4,256,512]{1,2,0:T(8,128)(2,1)}, u32[]{:S(2)}, u32[]{:S(2)}) async-start(bf16[4,256,512]{1,2,0:T(8,128)(2,1)} %stack.16), calls=%async_computation | async-start | bytes 2097152 | tf_op jit(solution)/shard_map/all_to_all | solution.py:15
  76.2 123.1 %reduce-scatter.11.cloned.1.call-start = ((), (), s32[]{:S(2)}) async-start(), calls=%async_computation.11 | async-start | bytes 1310720 | tf_op jit(solution)/shard_map/reduce_scatter | solution.py:146
  76.5 4.0 %copy-start.102 = (bf16[2048,512]{1,0:T(8,128)(2,1)S(1)}, bf16[2048,512]{1,0:T(8,128)(2,1)}, u32[]{:S(2)}) copy-start(bf16[2048,512]{1,0:T(8,128)(2,1)} %param.21) | copy-start | bytes 6291460
  78.3 40.1 %copy-start.17 = (bf16[256,256]{1,0:T(8,128)(2,1)}, bf16[256,256]{1,0:T(8,128)(2,1)S(1)}, u32[]{:S(2)}) copy-start(bf16[256,256]{1,0:T(8,128)(2,1)S(1)} %convolution_convert_fusion.13) | copy-start | bytes 393220
  88.5 3.9 %copy-start.103 = (bf16[2048,512]{1,0:T(8,128)(2,1)S(1)}, bf16[2048,512]{1,0:T(8,128)(2,1)}, u32[]{:S(2)}) copy-start(bf16[2048,512]{1,0:T(8,128)(2,1)} %param.21) | copy-start | bytes 6291460
  92.5 4.0 %copy-start.74 = (f32[256,16]{0,1:T(8,128)S(1)}, f32[256,16]{0,1:T(8,128)}, u32[]{:S(2)}) copy-start(f32[256,16]{0,1:T(8,128)} %fusion.198) | copy-start | bytes 49156
  95.9 19.9 %copy-start.11 = (f32[4,64,256]{2,1,0:T(8,128)}, f32[4,64,256]{2,1,0:T(8,128)S(1)}, u32[]{:S(2)}) copy-start(f32[4,64,256]{2,1,0:T(8,128)S(1)} %reduce_window_sum.67) | copy-start | bytes 786436
  97.2 19.8 %copy-start.13 = (f32[4,64,256]{2,1,0:T(8,128)}, f32[4,64,256]{2,1,0:T(8,128)S(1)}, u32[]{:S(2)}) copy-start(f32[4,64,256]{2,1,0:T(8,128)S(1)} %reduce_window_sum.68) | copy-start | bytes 786436
  106.3 8.3 %copy-start.15 = (f32[4,64,256]{2,1,0:T(8,128)}, f32[4,64,256]{2,1,0:T(8,128)S(1)}, u32[]{:S(2)}) copy-start(f32[4,64,256]{2,1,0:T(8,128)S(1)} %reduce_window_sum.64) | copy-start | bytes 786436
  119.8 3.6 %copy-start.97 = (f32[1,256]{1,0:T(1,128)S(1)}, f32[1,256]{1,0:T(1,128)}, u32[]{:S(2)}) copy-start(f32[1,256]{1,0:T(1,128)} %get-tuple-element.90) | copy-start | bytes 3076
  123.5 19.5 %copy-start.5 = (bf16[2048,256]{1,0:T(8,128)(2,1)S(1)}, bf16[2048,256]{1,0:T(8,128)(2,1)}, u32[]{:S(2)}) copy-start(bf16[2048,256]{1,0:T(8,128)(2,1)} %param.19) | copy-start | bytes 3145732
  125.0 20.5 %copy-start.67 = (s32[4,64]{1,0:T(4,128)S(1)}, s32[4,64]{1,0:T(4,128)}, u32[]{:S(2)}) copy-start(s32[4,64]{1,0:T(4,128)} %copy-done.66) | copy-start | bytes 3076
  125.0 20.5 %copy-start.72 = (f32[4,256]{1,0:T(4,128)S(1)}, f32[4,256]{1,0:T(4,128)}, u32[]{:S(2)}) copy-start(f32[4,256]{1,0:T(4,128)} %get-tuple-element.137) | copy-start | bytes 12292
  127.6 17.8 %copy-start.14 = (f32[4,64,256]{2,1,0:T(8,128)S(1)}, f32[4,64,256]{2,1,0:T(8,128)}, u32[]{:S(2)}) copy-start(f32[4,64,256]{2,1,0:T(8,128)} %copy-done.13) | copy-start | bytes 786436
  127.6 17.8 %copy-start.22 = (bf16[256,256]{1,0:T(8,128)(2,1)S(1)}, bf16[256,256]{1,0:T(8,128)(2,1)}, u32[]{:S(2)}) copy-start(bf16[256,256]{1,0:T(8,128)(2,1)} %convolution_convert_fusion.11) | copy-start | bytes 393220
  128.6 17.3 %copy-start.45 = (f32[1,256,512]{2,1,0:T(8,128)S(1)}, f32[1,256,512]{2,1,0:T(8,128)}, u32[]{:S(2)}) copy-start(f32[1,256,512]{2,1,0:T(8,128)} %get-tuple-element.45) | copy-start | bytes 1572868
  128.7 17.3 %copy-start.46 = (f32[1,256,512]{2,1,0:T(8,128)S(1)}, f32[1,256,512]{2,1,0:T(8,128)}, u32[]{:S(2)}) copy-start(f32[1,256,512]{2,1,0:T(8,128)} %get-tuple-element.46) | copy-start | bytes 1572868
  128.7 17.3 %copy-start.47 = (f32[1,256,512]{2,1,0:T(8,128)S(1)}, f32[1,256,512]{2,1,0:T(8,128)}, u32[]{:S(2)}) copy-start(f32[1,256,512]{2,1,0:T(8,128)} %get-tuple-element.47) | copy-start | bytes 1572868
  128.7 17.3 %copy-start.48 = (f32[1,256,512]{2,1,0:T(8,128)S(1)}, f32[1,256,512]{2,1,0:T(8,128)}, u32[]{:S(2)}) copy-start(f32[1,256,512]{2,1,0:T(8,128)} %get-tuple-element.48) | copy-start | bytes 1572868
  128.7 17.3 %copy-start.100 = (f32[4,64]{1,0:T(4,128)S(1)}, f32[4,64]{1,0:T(4,128)}, u32[]{:S(2)}) copy-start(f32[4,64]{1,0:T(4,128)} %get-tuple-element.83) | copy-start | bytes 3076
  128.7 19.1 %collective-permute-start.3 = (bf16[258,512]{1,0:T(8,128)(2,1)S(1)}, bf16[258,512]{1,0:T(8,128)(2,1)S(1)}, u32[]{:S(2)}, u32[]{:S(2)}) collective-permute-start(bf16[258,512]{1,0:T(8,128)(2,1)S(1)} %pad_maximum_fusion.1), channel_id=1, source_target_pairs={{0,16},{4,20},{8,24},{12,28},{16,32},{20,36},{24,40},{28,44},{32,4... | collective-permute-start | bytes 792584 | tf_op jit(solution)/shard_map/ppermute | solution.py:21
  134.6 13.7 %collective-permute-start.2 = (bf16[258,512]{1,0:T(8,128)(2,1)S(1)}, bf16[258,512]{1,0:T(8,128)(2,1)S(1)}, u32[]{:S(2)}, u32[]{:S(2)}) collective-permute-start(bf16[258,512]{1,0:T(8,128)(2,1)S(1)} %pad_maximum_fusion.1), channel_id=1, source_target_pairs={{0,12},{4,16},{8,20},{12,24},{16,28},{20,32},{24,36},{28,40},{32,4... | collective-permute-start | bytes 792584 | tf_op jit(solution)/shard_map/ppermute | solution.py:21
  136.0 15.2 %collective-permute-start.1 = (bf16[258,512]{1,0:T(8,128)(2,1)S(1)}, bf16[258,512]{1,0:T(8,128)(2,1)S(1)}, u32[]{:S(2)}, u32[]{:S(2)}) collective-permute-start(bf16[258,512]{1,0:T(8,128)(2,1)S(1)} %pad_maximum_fusion.1), channel_id=1, source_target_pairs={{0,8},{4,12},{8,16},{12,20},{16,24},{20,28},{24,32},{28,36},{32,40... | collective-permute-start | bytes 792584 | tf_op jit(solution)/shard_map/ppermute | solution.py:21
  138.9 14.9 %collective-permute-start = (bf16[258,512]{1,0:T(8,128)(2,1)S(1)}, bf16[258,512]{1,0:T(8,128)(2,1)S(1)}, u32[]{:S(2)}, u32[]{:S(2)}) collective-permute-start(bf16[258,512]{1,0:T(8,128)(2,1)S(1)} %pad_maximum_fusion.1), channel_id=1, source_target_pairs={{0,4},{4,8},{8,12},{12,16},{16,20},{20,24},{24,28},{28,32},{32,36}... | collective-permute-start | bytes 792584 | tf_op jit(solution)/shard_map/ppermute | solution.py:21
  146.0 11.2 %copy-start.59 = (s32[8,128]{1,0:T(8,128)S(1)}, s32[8,128]{1,0:T(8,128)}, u32[]{:S(2)}) copy-start(s32[8,128]{1,0:T(8,128)} %copy-done.58) | copy-start | bytes 12292
  146.0 11.2 %copy-start.95 = (s32[8]{0:T(128)S(1)}, s32[8]{0:T(128)}, u32[]{:S(2)}) copy-start(s32[8]{0:T(128)} %copy-done.94) | copy-start | bytes 100
  147.8 7.4 %copy-start.52 = (bf16[258,512]{1,0:T(8,128)(2,1)}, bf16[258,512]{1,0:T(8,128)(2,1)S(1)}, u32[]{:S(2)}) copy-start(bf16[258,512]{1,0:T(8,128)(2,1)S(1)} %collective-permute-done.3) | copy-start | bytes 792580
  157.2 3.8 %copy-start.53 = (bf16[258,512]{1,0:T(8,128)(2,1)S(1)}, bf16[258,512]{1,0:T(8,128)(2,1)}, u32[]{:S(2)}) copy-start(bf16[258,512]{1,0:T(8,128)(2,1)} %copy-done.52) | copy-start | bytes 792580
  163.2 4.6 %copy-start.4 = (bf16[4,256,512]{1,2,0:T(8,128)(2,1)S(1)}, bf16[4,256,512]{1,2,0:T(8,128)(2,1)}, u32[]{:S(2)}) copy-start(bf16[4,256,512]{1,2,0:T(8,128)(2,1)} %copy-done.2) | copy-start | bytes 3145732
  167.8 51.6 %reduce-scatter.9.cloned.1.call-start = ((), (), s32[]{:S(2)}) async-start(), calls=%async_computation.10 | async-start | bytes 1310720 | tf_op jit(solution)/shard_map/reduce_scatter | solution.py:146
  178.7 66.6 %reduce-scatter.7.cloned.1.call-start = ((), (), s32[]{:S(2)}) async-start(), calls=%async_computation.9 | async-start | bytes 1310720 | tf_op jit(solution)/shard_map/reduce_scatter | solution.py:146
  185.2 4.7 %copy-start.6 = (bf16[2048,256]{1,0:T(8,128)(2,1)S(1)}, bf16[2048,256]{1,0:T(8,128)(2,1)}, u32[]{:S(2)}) copy-start(bf16[2048,256]{1,0:T(8,128)(2,1)} %param.19) | copy-start | bytes 3145732
  189.8 81.1 %reduce-scatter.5.cloned.1.call-start = ((), (), s32[]{:S(2)}) async-start(), calls=%async_computation.8 | async-start | bytes 1310720 | tf_op jit(solution)/shard_map/reduce_scatter | solution.py:146
  (72 other events, 138.6 us)
Sparse Core Ops, SparseCore 0:
  167.9 25.5 reduce-scatter.10
  195.9 23.4 reduce-scatter.8
  221.8 23.4 reduce-scatter.6
  247.5 23.3 reduce-scatter.4
